TPU v7x, 256 devices: a whole 4x4x8 slice. The times are simulated.
256 devices in a mesh: ctx: 8 (over z_lo, core), head: 8 (over x, z_hi), rep: 4 (over y).
Axes of the slice: x: 4, y: 4, z: 8 (z_hi: 2, z_lo: 4; z = z_hi * 4 + z_lo), core: 2. Of those that a mesh axis runs over, the one named last changes fastest.
Arguments:
- queries: bfloat16 [4, 1024, 8192], P('rep', 'ctx', 'head'), may hold values from -12 to 12
- keys: bfloat16 [4, 1024, 1024], P('rep', 'ctx', 'head'), may hold values from -12 to 12
- values: bfloat16 [4, 1024, 1024], P('rep', 'ctx', 'head'), may hold values from -6 to 6
- grad_out: bfloat16 [4, 1024, 8192], P('rep', 'ctx', 'head'), may hold values from -90 to 90
- segment_ids: int32 [4, 1024], P('rep'), may hold values from 0 to 15, never falling along the last dimension, each value on 1 to 512 neighbouring positions
- head_mask: float32 [64], P('head'), may hold values from 0.25 to 1
- ablated_heads: int32 [8], replicated, may hold values from 0 to 63, as said below
- w_query: bfloat16 [8192, 8192], P(('ctx', 'rep'), 'head'), may hold values from -0.0625 to 0.0625
- w_key: bfloat16 [8192, 1024], P(('ctx', 'rep'), 'head'), may hold values from -0.0625 to 0.0625
- w_value: bfloat16 [8192, 1024], P(('ctx', 'rep'), 'head'), may hold values from -0.0625 to 0.0625
Outputs:
- input_grad: bfloat16 [4, 1024, 8192], P('rep', None, ('ctx', 'head'))
- mask_grad: float32 [64], P('head')
Inputs may be any that keep to these rules, and one draw needn't show every extreme that they name: `ablated_heads`: the 8 entries are all different.
All inputs are finite; a program needn't handle non-finite values.
Results may differ from a plain program's by a relative error of at most 0.02.
Values may be sent and summed in bfloat16 or wider, within the bound.
No kernel may reach another device: no remote copies, remote signals or barrier semaphores. Data moves between devices by JAX's collectives and lax.ppermute only.
A program may use at most 128 MiB of HBM per device.

v0:
```python
import math

import jax
import jax.numpy as jnp
from jax import lax
from jax.sharding import PartitionSpec as P

DH = 128


NEG_FILL = -1e30


def shifted(block, axis, distance):
    devices = range(lax.axis_size(axis))
    route = [((i - distance) % len(devices), i) for i in devices]
    return lax.ppermute(block, axis, route)


def times_rows(left, right):
    return lax.dot_general(
        left, right, (((1,), (1,)), ((), ())), preferred_element_type=jnp.float32
    )


def block_scores(query_blocks, key_piece, query_pos, query_seg, key_seg, key_start):
    key_count = key_piece.shape[0]
    key_pos = key_start + jnp.arange(key_count, dtype=jnp.int32)
    allowed = (key_pos[None, :] <= query_pos[:, None]) & (key_seg[None, :] == query_seg[:, None])
    score_scale = 1.0 / math.sqrt(query_blocks.shape[-1])
    scores = (
        jnp.einsum("gjtc,kgc->gjtk", query_blocks, key_piece, preferred_element_type=jnp.float32)
        * score_scale
    )
    return (jnp.where(allowed, scores, NEG_FILL), allowed)


def rotate(key_value):
    return shifted(key_value, "ctx", -1)


def on_device(
    queries, keys, values, grad_out, segment_ids, head_mask, ablated_heads, w_query, w_key, w_value
):
    rows_dev = queries.shape[1]
    groups = keys.shape[2] // DH
    local_heads = head_mask.shape[0]
    per_group = local_heads // groups
    block_count = lax.axis_size("ctx")
    my_block = lax.axis_index("ctx")
    seq_len = block_count * rows_dev
    score_scale = 1.0 / math.sqrt(DH)
    all_seg = segment_ids[0]
    query_pos = my_block * rows_dev + jnp.arange(rows_dev, dtype=jnp.int32)
    query_seg = lax.dynamic_slice_in_dim(all_seg, my_block * rows_dev, rows_dev, 0)
    query_blocks = queries[0].reshape(rows_dev, groups, per_group, DH).transpose(1, 2, 0, 3)
    grad_blocks = grad_out[0].reshape(rows_dev, groups, per_group, DH).transpose(1, 2, 0, 3)
    head_ids = lax.axis_index("head") * local_heads + jnp.arange(local_heads, dtype=jnp.int32)
    ablate = jnp.any(head_ids[:, None] == ablated_heads[None, :], axis=1)
    head_scale = jnp.where(ablate, 0.0, head_mask).reshape(groups, per_group)
    key_value = jnp.stack([keys, values])

    def block_source(step_index):
        source = (my_block + step_index) % block_count
        key_start = source * rows_dev
        return (key_start, lax.dynamic_slice_in_dim(all_seg, key_start, rows_dev, 0))

    def forward_step(step_index, carried):
        moving, row_max, denominator, weighted = carried
        key_start, key_seg = block_source(step_index)
        softmax_state = (row_max, denominator, weighted)
        old_max, old_sum, old_weighted = softmax_state
        key_piece = moving[0, 0].reshape(rows_dev, groups, DH)
        value_piece = moving[1, 0].reshape(rows_dev, groups, DH)
        scores, allowed = block_scores(
            query_blocks, key_piece, query_pos, query_seg, key_seg, key_start
        )
        new_max = jnp.maximum(old_max, jnp.max(scores, axis=-1))
        exponent = jnp.where(allowed, jnp.exp(scores - new_max[..., None]), 0.0)
        rescale = jnp.exp(old_max - new_max)
        new_sum = old_sum * rescale + jnp.sum(exponent, axis=-1)
        new_weighted = old_weighted * rescale[..., None] + jnp.einsum(
            "gjtk,kgc->gjtc",
            exponent.astype(jnp.bfloat16),
            value_piece,
            preferred_element_type=jnp.float32,
        )
        softmax_state = (new_max, new_sum, new_weighted)
        return (rotate(moving),) + softmax_state

    start_max = jnp.full((groups, per_group, rows_dev), NEG_FILL, jnp.float32)
    start_sum = jnp.zeros((groups, per_group, rows_dev), jnp.float32)
    start_weighted = jnp.zeros((groups, per_group, rows_dev, DH), jnp.float32)
    forward_end = lax.fori_loop(
        0, block_count, forward_step, (key_value, start_max, start_sum, start_weighted)
    )
    row_max, denominator, weighted = (forward_end[1], forward_end[2], forward_end[3])
    log_total = row_max + jnp.log(denominator)
    head_out = (weighted / denominator[..., None]).astype(jnp.bfloat16)
    out_grad = (head_scale[:, :, None, None] * grad_blocks.astype(jnp.float32)).astype(jnp.bfloat16)
    out_dot = jnp.sum(out_grad.astype(jnp.float32) * head_out.astype(jnp.float32), axis=-1)

    def backward_step(step_index, carried):
        moving, key_grads, query_grad = carried
        key_start, key_seg = block_source(step_index)
        grad_state = (key_grads, query_grad)
        old_keys, old_query = grad_state
        key_piece = moving[0, 0].reshape(rows_dev, groups, DH)
        value_piece = moving[1, 0].reshape(rows_dev, groups, DH)
        scores, allowed = block_scores(
            query_blocks, key_piece, query_pos, query_seg, key_seg, key_start
        )
        probability = jnp.where(allowed, jnp.exp(scores - log_total[..., None]), 0.0)
        prob_grad = jnp.einsum(
            "gjtc,kgc->gjtk", out_grad, value_piece, preferred_element_type=jnp.float32
        )
        score_grad = (probability * (prob_grad - out_dot[..., None])).astype(jnp.bfloat16)
        value_term = jnp.einsum(
            "gjtk,gjtc->kgc",
            probability.astype(jnp.bfloat16),
            out_grad,
            preferred_element_type=jnp.float32,
        )
        key_term = (
            jnp.einsum(
                "gjtk,gjtc->kgc", score_grad, query_blocks, preferred_element_type=jnp.float32
            )
            * score_scale
        )
        new_query = (
            old_query
            + jnp.einsum(
                "gjtk,kgc->gjtc", score_grad, key_piece, preferred_element_type=jnp.float32
            )
            * score_scale
        )
        new_terms = jnp.stack([key_term, value_term]).reshape(old_keys.shape)
        grad_state = (old_keys + new_terms, new_query)
        passed = shifted(grad_state[0].astype(jnp.bfloat16), "ctx", -1).astype(jnp.float32)
        return (rotate(moving), passed, grad_state[1])

    backward_end = lax.fori_loop(
        0,
        block_count,
        backward_step,
        (
            key_value,
            jnp.zeros(key_value.shape, jnp.float32),
            jnp.zeros(query_blocks.shape, jnp.float32),
        ),
    )
    key_grads, query_grad = (backward_end[1], backward_end[2])
    query_rows = (
        query_grad.astype(jnp.bfloat16).transpose(2, 0, 1, 3).reshape(1, rows_dev, local_heads * DH)
    )
    key_rows = key_grads[0].astype(jnp.bfloat16)
    value_rows = key_grads[1].astype(jnp.bfloat16)
    mask_terms = jnp.sum(
        head_out.astype(jnp.float32) * grad_blocks.astype(jnp.float32), axis=(2, 3)
    ).reshape(local_heads)
    mask_grad = lax.psum(mask_terms, ("ctx", "rep")) / math.sqrt(lax.axis_size("rep") * seq_len)
    query_piece, key_piece, value_piece = lax.all_gather(
        (w_query, w_key, w_value), ("ctx", "rep"), axis=0, tiled=True
    )
    product = times_rows(query_rows[0], query_piece) + times_rows(key_rows[0], key_piece)
    product = product + times_rows(value_rows[0], value_piece)
    partial_value = product.astype(jnp.bfloat16)
    heads_count = lax.axis_size("head")
    columns = partial_value.shape[1]
    blocks = partial_value.reshape(
        rows_dev, block_count, heads_count, columns // (block_count * heads_count)
    )
    widened = lax.optimization_barrier(blocks).astype(jnp.float32)
    summed = lax.psum_scatter(widened.astype(jnp.bfloat16), "head", scatter_dimension=2, tiled=True)
    arrived = lax.all_to_all(summed, "ctx", split_axis=1, concat_axis=0, tiled=True)
    result = arrived.reshape(1, seq_len, -1)
    return (result, mask_grad)


def solution(mesh):
    placed = (
        P("rep", "ctx", "head"),
        P("rep", "ctx", "head"),
        P("rep", "ctx", "head"),
        P("rep", "ctx", "head"),
        P("rep", None),
        P("head"),
        P(),
        P(("ctx", "rep"), "head"),
        P(("ctx", "rep"), "head"),
        P(("ctx", "rep"), "head"),
    )
    return jax.shard_map(
        on_device,
        mesh=mesh,
        in_specs=placed,
        out_specs=(P("rep", None, ("ctx", "head")), P("head")),
        check_vma=False,
    )
```

profile of v0, /device:TPU:4, one launch (start us, length us, event | category | flops | bytes accessed | tf_op | source)
XLA Modules:
  0.0 596.3 jit_solution(3280781085750209755)
XLA Ops:
  7.9 0.7 all-gather.6.cloned.1.call-update
  8.7 0.7 all-gather.8.cloned.1.call-update
  9.5 1.1 copy.68
  10.8 0.8 pad_maximum_fusion
  12.3 48.7 %while.42 = (s32[]{:T(128)}, bf16[2,1,128,128]{3,2,1,0:T(8,128)(2,1)S(1)}, f32[1,8,128]{2,1,0:T(8,128)S(1)}, f32[1,8,128]{2,1,0:T(8,128)S(1)}, f32[1,8,128,128]{...) while((s32[]{:T(128)}, ...), condition=%wide.region_3.4_spmd.clone, body=%wide.region_0.3_spmd.clone.sunk | while | flops 68737296 | bytes 3477884 | solution.py:94
  12.3 4.1 collective-permute-start
  16.4 0.8 dynamic_slice.32
  18.3 3.6 collective-permute-start
  21.9 0.8 dynamic_slice.32
  23.8 3.6 collective-permute-start
  27.4 0.8 dynamic_slice.32
  29.1 0.7 collective-permute-done
  29.8 3.7 collective-permute-start
  33.5 0.8 dynamic_slice.32
  35.2 0.8 collective-permute-done
  36.0 3.7 collective-permute-start
  39.8 0.8 dynamic_slice.32
  41.5 0.8 collective-permute-done
  42.3 3.7 collective-permute-start
  46.0 0.8 dynamic_slice.32
  47.7 0.8 collective-permute-done
  48.6 3.7 collective-permute-start
  52.3 0.8 dynamic_slice.32
  54.0 0.8 collective-permute-done
  54.7 3.7 collective-permute-start
  58.5 0.8 dynamic_slice.32
  60.2 0.8 collective-permute-done
  62.1 67.9 %while.43 = (s32[]{:T(128)}, bf16[2,1,128,128]{3,2,1,0:T(8,128)(2,1)S(1)}, f32[2,1,128,128]{3,2,0,1:T(8,128)S(1)}, f32[1,8,128,128]{3,2,1,0:T(8,128)S(1)}, s32[]...) while((s32[]{:T(128)}, ...), condition=%wide.region_7.8_spmd.clone, body=%wide.region_6.7_spmd.clone.sunk | while | flops 169443600 | bytes 5910963 | solution.py:142
  62.1 3.8 collective-permute-start.1
  65.9 0.8 dynamic_slice.33
  68.3 2.3 collective-permute-done.2
  70.7 3.8 collective-permute-start.1
  74.4 0.8 dynamic_slice.33
  76.9 2.3 collective-permute-done.2
  79.2 3.8 collective-permute-start.1
  83.0 0.8 dynamic_slice.33
  85.4 2.3 collective-permute-done.2
  87.7 3.8 collective-permute-start.1
  91.5 0.8 dynamic_slice.33
  94.0 2.3 collective-permute-done.2
  96.3 3.8 collective-permute-start.1
  100.1 0.8 dynamic_slice.33
  102.5 2.3 collective-permute-done.2
  104.8 3.8 collective-permute-start.1
  108.6 0.8 dynamic_slice.33
  111.0 2.3 collective-permute-done.2
  113.4 3.8 collective-permute-start.1
  117.2 0.8 dynamic_slice.33
  119.6 2.3 collective-permute-done.2
  121.9 3.8 collective-permute-start.1
  125.7 0.8 dynamic_slice.33
  128.1 1.6 collective-permute-done.2
  130.2 1.1 all-gather.4.cloned.1.call-done
  131.2 13.4 %fusion.49 = f32[128,8192]{1,0:T(8,128)} fusion(bf16[128,1024]{0,1:T(8,128)(2,1)S(1)} %bitcast.192, bf16[8192,1024]{1,0:T(8,128)(2,1)} %all-gather.4.cloned.1.call-done), kind=kOutput, calls=%fused_computation.83 | convolution fusion | flops 2147483648 | bytes 21233664 | tf_op jit(solution)/shard_map/dot_general | solution.py:21
  144.7 73.3 %all-gather.6.cloned.1.call-done = bf16[8192,128]{1,0:T(8,128)(2,1)} async-done(((bf16[256,128]{1,0:T(8,128)(2,1)}), bf16[8192,128]{1,0:T(8,128)(2,1)}) %all-gather.6.cloned.1.call-update) | async-done | bytes 2097168 | tf_op jit(solution)/shard_map/all_gather | solution.py:162
  218.0 5.5 convolution_add_fusion.1
  223.4 83.2 %all-gather.8.cloned.1.call-done = bf16[8192,128]{1,0:T(8,128)(2,1)} async-done(((bf16[256,128]{1,0:T(8,128)(2,1)}), bf16[8192,128]{1,0:T(8,128)(2,1)}) %all-gather.8.cloned.1.call-update) | async-done | bytes 2097168 | tf_op jit(solution)/shard_map/all_gather | solution.py:162
  306.6 3.5 fusion.43
  310.8 2.7 copy.75
  314.7 194.9 %all-reduce.3.cloned.1.call-done = bf16[128,8,8,128]{3,0,2,1:T(8,128)(2,1)} async-done(((bf16[128,8,8,128]{3,0,2,1:T(8,128)(2,1)}), bf16[128,8,8,128]{3,0,2,1:T(8,128)(2,1)}) %all-reduce.3.cloned.1.call-update) | async-done | bytes 2097168
  509.7 2.3 constant_dynamic-slice_fusion
  512.0 3.4 all-to-all-start
  515.4 72.9 %psum.7 = f32[8]{0:T(128)S(1)} all-reduce(f32[8]{0:T(128)S(1)} %get-tuple-element.728), channel_id=1, replica_groups=mesh['ctx'=8,'head'=8,'rep'=4] {'ctx','rep'}, use_global_device_ids=true, to_apply=%region_10.11 | all-reduce | flops 8 | bytes 64 | tf_op jit(solution)/shard_map/psum | solution.py:161
  589.0 0.7 copy.77
  (224 shorter events, 26.1 us)
Async XLA Ops:
  7.2 124.1 %all-gather.4.cloned.1.call-start = ((), (), s32[]{:S(2)}) async-start(), calls=%async_computation.1 | async-start | bytes 17301504 | tf_op jit(solution)/shard_map/all_gather | solution.py:162
  7.9 210.1 %all-gather.6.cloned.1.call-start = ((), (), s32[]{:S(2)}) async-start(), calls=%async_computation.2 | async-start | bytes 2162688 | tf_op jit(solution)/shard_map/all_gather | solution.py:162
  8.6 298.0 %all-gather.8.cloned.1.call-start = ((), (), s32[]{:S(2)}) async-start(), calls=%async_computation.3 | async-start | bytes 2162688 | tf_op jit(solution)/shard_map/all_gather | solution.py:162
  9.4 500.3 %all-reduce.3.cloned.1.call-start = ((), (), s32[]{:S(2)}) async-start(), calls=%async_computation.4 | async-start | bytes 4194304
  12.3 48.9 %copy-start = (bf16[1,128,1024]{2,1,0:T(8,128)(2,1)S(1)}, bf16[1,128,1024]{2,1,0:T(8,128)(2,1)}, u32[]{:S(2)}) copy-start(bf16[1,128,1024]{2,1,0:T(8,128)(2,1)} %param.17) | copy-start | bytes 786436
  12.3 49.1 %copy-start.1 = (s32[8]{0:T(128)S(1)}, s32[8]{0:T(128)}, u32[]{:S(2)}) copy-start(s32[8]{0:T(128)} %param.20) | copy-start | bytes 100
  12.3 49.3 %copy-start.2 = (f32[8]{0:T(128)S(1)}, f32[8]{0:T(128)}, u32[]{:S(2)}) copy-start(f32[8]{0:T(128)} %param.19) | copy-start | bytes 100
  12.3 6.0 %collective-permute-start = (bf16[2,1,128,128]{3,2,1,0:T(8,128)(2,1)S(1)}, bf16[2,1,128,128]{3,2,1,0:T(8,128)(2,1)S(1)}, u32[]{:S(2)}, u32[]{:S(2)}) collective-permute-start(bf16[2,1,128,128]{3,2,1,0:T(8,128)(2,1)S(1)} %copy.92), channel_id=1, source_target_pairs={{32,0},{64,32},{96,64},{128,96},{160,128},{192,160},{224,192},{0,2... | collective-permute-start | bytes 196616 | tf_op jit(solution)/shard_map/while/body/eval_jaxpr/ppermute | solution.py:17
  18.3 5.5 collective-permute-start
  23.8 6.0 %collective-permute-start = (bf16[2,1,128,128]{3,2,1,0:T(8,128)(2,1)S(1)}, bf16[2,1,128,128]{3,2,1,0:T(8,128)(2,1)S(1)}, u32[]{:S(2)}, u32[]{:S(2)}) collective-permute-start(bf16[2,1,128,128]{3,2,1,0:T(8,128)(2,1)S(1)} %copy.92), channel_id=1, source_target_pairs={{32,0},{64,32},{96,64},{128,96},{160,128},{192,160},{224,192},{0,2... | collective-permute-start | bytes 196616 | tf_op jit(solution)/shard_map/while/body/eval_jaxpr/ppermute | solution.py:17
  29.8 6.2 %collective-permute-start = (bf16[2,1,128,128]{3,2,1,0:T(8,128)(2,1)S(1)}, bf16[2,1,128,128]{3,2,1,0:T(8,128)(2,1)S(1)}, u32[]{:S(2)}, u32[]{:S(2)}) collective-permute-start(bf16[2,1,128,128]{3,2,1,0:T(8,128)(2,1)S(1)} %copy.92), channel_id=1, source_target_pairs={{32,0},{64,32},{96,64},{128,96},{160,128},{192,160},{224,192},{0,2... | collective-permute-start | bytes 196616 | tf_op jit(solution)/shard_map/while/body/eval_jaxpr/ppermute | solution.py:17
  36.0 6.3 %collective-permute-start = (bf16[2,1,128,128]{3,2,1,0:T(8,128)(2,1)S(1)}, bf16[2,1,128,128]{3,2,1,0:T(8,128)(2,1)S(1)}, u32[]{:S(2)}, u32[]{:S(2)}) collective-permute-start(bf16[2,1,128,128]{3,2,1,0:T(8,128)(2,1)S(1)} %copy.92), channel_id=1, source_target_pairs={{32,0},{64,32},{96,64},{128,96},{160,128},{192,160},{224,192},{0,2... | collective-permute-start | bytes 196616 | tf_op jit(solution)/shard_map/while/body/eval_jaxpr/ppermute | solution.py:17
  42.3 6.3 %collective-permute-start = (bf16[2,1,128,128]{3,2,1,0:T(8,128)(2,1)S(1)}, bf16[2,1,128,128]{3,2,1,0:T(8,128)(2,1)S(1)}, u32[]{:S(2)}, u32[]{:S(2)}) collective-permute-start(bf16[2,1,128,128]{3,2,1,0:T(8,128)(2,1)S(1)} %copy.92), channel_id=1, source_target_pairs={{32,0},{64,32},{96,64},{128,96},{160,128},{192,160},{224,192},{0,2... | collective-permute-start | bytes 196616 | tf_op jit(solution)/shard_map/while/body/eval_jaxpr/ppermute | solution.py:17
  48.6 6.2 %collective-permute-start = (bf16[2,1,128,128]{3,2,1,0:T(8,128)(2,1)S(1)}, bf16[2,1,128,128]{3,2,1,0:T(8,128)(2,1)S(1)}, u32[]{:S(2)}, u32[]{:S(2)}) collective-permute-start(bf16[2,1,128,128]{3,2,1,0:T(8,128)(2,1)S(1)} %copy.92), channel_id=1, source_target_pairs={{32,0},{64,32},{96,64},{128,96},{160,128},{192,160},{224,192},{0,2... | collective-permute-start | bytes 196616 | tf_op jit(solution)/shard_map/while/body/eval_jaxpr/ppermute | solution.py:17
  54.7 6.2 %collective-permute-start = (bf16[2,1,128,128]{3,2,1,0:T(8,128)(2,1)S(1)}, bf16[2,1,128,128]{3,2,1,0:T(8,128)(2,1)S(1)}, u32[]{:S(2)}, u32[]{:S(2)}) collective-permute-start(bf16[2,1,128,128]{3,2,1,0:T(8,128)(2,1)S(1)} %copy.92), channel_id=1, source_target_pairs={{32,0},{64,32},{96,64},{128,96},{160,128},{192,160},{224,192},{0,2... | collective-permute-start | bytes 196616 | tf_op jit(solution)/shard_map/while/body/eval_jaxpr/ppermute | solution.py:17
  62.1 8.5 %collective-permute-start.1 = (bf16[2,1,128,128]{3,2,1,0:T(8,128)(2,1)S(1)}, bf16[2,1,128,128]{3,2,1,0:T(8,128)(2,1)S(1)}, u32[]{:S(2)}, u32[]{:S(2)}) collective-permute-start(bf16[2,1,128,128]{3,2,1,0:T(8,128)(2,1)S(1)} %copy.106), channel_id=1, source_target_pairs={{32,0},{64,32},{96,64},{128,96},{160,128},{192,160},{224,192},{0,2... | collective-permute-start | bytes 196616 | tf_op jit(solution)/shard_map/while/body/eval_jaxpr/ppermute | solution.py:17
  67.9 2.7 collective-permute-start.2
  70.7 8.5 %collective-permute-start.1 = (bf16[2,1,128,128]{3,2,1,0:T(8,128)(2,1)S(1)}, bf16[2,1,128,128]{3,2,1,0:T(8,128)(2,1)S(1)}, u32[]{:S(2)}, u32[]{:S(2)}) collective-permute-start(bf16[2,1,128,128]{3,2,1,0:T(8,128)(2,1)S(1)} %copy.106), channel_id=1, source_target_pairs={{32,0},{64,32},{96,64},{128,96},{160,128},{192,160},{224,192},{0,2... | collective-permute-start | bytes 196616 | tf_op jit(solution)/shard_map/while/body/eval_jaxpr/ppermute | solution.py:17
  76.5 2.7 collective-permute-start.2
  79.2 8.5 %collective-permute-start.1 = (bf16[2,1,128,128]{3,2,1,0:T(8,128)(2,1)S(1)}, bf16[2,1,128,128]{3,2,1,0:T(8,128)(2,1)S(1)}, u32[]{:S(2)}, u32[]{:S(2)}) collective-permute-start(bf16[2,1,128,128]{3,2,1,0:T(8,128)(2,1)S(1)} %copy.106), channel_id=1, source_target_pairs={{32,0},{64,32},{96,64},{128,96},{160,128},{192,160},{224,192},{0,2... | collective-permute-start | bytes 196616 | tf_op jit(solution)/shard_map/while/body/eval_jaxpr/ppermute | solution.py:17
  85.0 2.7 collective-permute-start.2
  87.7 8.5 %collective-permute-start.1 = (bf16[2,1,128,128]{3,2,1,0:T(8,128)(2,1)S(1)}, bf16[2,1,128,128]{3,2,1,0:T(8,128)(2,1)S(1)}, u32[]{:S(2)}, u32[]{:S(2)}) collective-permute-start(bf16[2,1,128,128]{3,2,1,0:T(8,128)(2,1)S(1)} %copy.106), channel_id=1, source_target_pairs={{32,0},{64,32},{96,64},{128,96},{160,128},{192,160},{224,192},{0,2... | collective-permute-start | bytes 196616 | tf_op jit(solution)/shard_map/while/body/eval_jaxpr/ppermute | solution.py:17
  93.5 2.7 collective-permute-start.2
  96.3 8.5 %collective-permute-start.1 = (bf16[2,1,128,128]{3,2,1,0:T(8,128)(2,1)S(1)}, bf16[2,1,128,128]{3,2,1,0:T(8,128)(2,1)S(1)}, u32[]{:S(2)}, u32[]{:S(2)}) collective-permute-start(bf16[2,1,128,128]{3,2,1,0:T(8,128)(2,1)S(1)} %copy.106), channel_id=1, source_target_pairs={{32,0},{64,32},{96,64},{128,96},{160,128},{192,160},{224,192},{0,2... | collective-permute-start | bytes 196616 | tf_op jit(solution)/shard_map/while/body/eval_jaxpr/ppermute | solution.py:17
  102.1 2.7 collective-permute-start.2
  104.8 8.5 %collective-permute-start.1 = (bf16[2,1,128,128]{3,2,1,0:T(8,128)(2,1)S(1)}, bf16[2,1,128,128]{3,2,1,0:T(8,128)(2,1)S(1)}, u32[]{:S(2)}, u32[]{:S(2)}) collective-permute-start(bf16[2,1,128,128]{3,2,1,0:T(8,128)(2,1)S(1)} %copy.106), channel_id=1, source_target_pairs={{32,0},{64,32},{96,64},{128,96},{160,128},{192,160},{224,192},{0,2... | collective-permute-start | bytes 196616 | tf_op jit(solution)/shard_map/while/body/eval_jaxpr/ppermute | solution.py:17
  110.6 2.7 collective-permute-start.2
  113.4 8.5 %collective-permute-start.1 = (bf16[2,1,128,128]{3,2,1,0:T(8,128)(2,1)S(1)}, bf16[2,1,128,128]{3,2,1,0:T(8,128)(2,1)S(1)}, u32[]{:S(2)}, u32[]{:S(2)}) collective-permute-start(bf16[2,1,128,128]{3,2,1,0:T(8,128)(2,1)S(1)} %copy.106), channel_id=1, source_target_pairs={{32,0},{64,32},{96,64},{128,96},{160,128},{192,160},{224,192},{0,2... | collective-permute-start | bytes 196616 | tf_op jit(solution)/shard_map/while/body/eval_jaxpr/ppermute | solution.py:17
  119.2 2.7 collective-permute-start.2
  121.9 7.9 %collective-permute-start.1 = (bf16[2,1,128,128]{3,2,1,0:T(8,128)(2,1)S(1)}, bf16[2,1,128,128]{3,2,1,0:T(8,128)(2,1)S(1)}, u32[]{:S(2)}, u32[]{:S(2)}) collective-permute-start(bf16[2,1,128,128]{3,2,1,0:T(8,128)(2,1)S(1)} %copy.106), channel_id=1, source_target_pairs={{32,0},{64,32},{96,64},{128,96},{160,128},{192,160},{224,192},{0,2... | collective-permute-start | bytes 196616 | tf_op jit(solution)/shard_map/while/body/eval_jaxpr/ppermute | solution.py:17
  127.7 2.1 collective-permute-start.2
  313.5 0.7 copy-start.3
  512.0 76.8 %all-to-all-start = ((bf16[128,8,1,128]{3,0,2,1:T(8,128)(2,1)}), bf16[128,8,1,128]{3,0,2,1:T(8,128)(2,1)S(1)}, u32[]{:S(2)}, u32[]{:S(2)}) async-start(bf16[128,8,1,128]{3,0,2,1:T(8,128)(2,1)} %constant_dynamic-slice_fusion), calls=%async_computation | async-start | bytes 524288 | tf_op jit(solution)/shard_map/all_to_all | solution.py:175
Sparse Core Ops, SparseCore 0:
  9.8 121.4 all-gather.3
  133.0 84.8 all-gather.5
  219.8 86.8 all-gather.7
  313.6 196.0 all-reduce.2
where the time goes:
time: 597 us; the launch traced here: 596 us
  waiting for transfers between devices  377 us (63%)
  blocking collectives  72.9 us (12%)
  starting transfers between devices  64.8 us (11%)
  matrix products  38.4 us (6%)
  local copies, waits for them, and re-layouts  22.7 us (4%)
  between operations  14 us (2%)
    unnamed x5, waiting for transfers between devices  197 us
    all_gather x3, waiting for transfers between devices, on_device(): lax.all_gather((w_query, w_key, w_value), ('ctx', 'rep'), axis=0, tiled=T...  158 us
    psum x1, blocking collectives, on_device(): lax.psum(mask_terms, ('ctx', 'rep'))  72.9 us
    ppermute x24, starting transfers between devices, shifted(): return lax.ppermute(block, axis, route)  61.3 us
    ppermute x24, waiting for transfers between devices, shifted(): return lax.ppermute(block, axis, route)  22.8 us
    dot_general x3, matrix products, times_rows(): lax.dot_general(left, right, (((1,), (1,)), ((), ())), preferred_element_...  22.4 us
    dynamic_slice x16, local copies, waits for them, and re-layouts, block_source(): lax.dynamic_slice_in_dim(all_seg, key_start, rows_dev, 0)  12.2 us
  transfers between devices with their start and end apart: 29, of which 20 were waited for; matrix products, arithmetic and copies ran while one was open for 9% of the time, Pallas kernels for 0%

commit v1 on v0

v1 whole, which is shorter than its diff:
```python
import math

import jax
import jax.numpy as jnp
from jax import lax
from jax.sharding import PartitionSpec as P

DH = 128


NEG_FILL = -1e30


def on_device(
    queries, keys, values, grad_out, segment_ids, head_mask, ablated_heads, w_query, w_key, w_value
):
    rows_dev = queries.shape[1]
    groups = keys.shape[2] // DH
    local_heads = head_mask.shape[0]
    per_group = local_heads // groups
    block_count = lax.axis_size("ctx")
    my_block = lax.axis_index("ctx")
    seq_len = block_count * rows_dev
    score_scale = 1.0 / math.sqrt(DH)
    all_seg = segment_ids[0]
    query_pos = my_block * rows_dev + jnp.arange(rows_dev, dtype=jnp.int32)
    query_seg = lax.dynamic_slice_in_dim(all_seg, my_block * rows_dev, rows_dev, 0)
    key_pos = jnp.arange(seq_len, dtype=jnp.int32)
    allowed = (key_pos[None, :] <= query_pos[:, None]) & (all_seg[None, :] == query_seg[:, None])

    query_heads = queries[0].reshape(rows_dev, local_heads, DH).transpose(1, 0, 2)
    grad_heads = grad_out[0].reshape(rows_dev, local_heads, DH).transpose(1, 0, 2)
    head_ids = lax.axis_index("head") * local_heads + jnp.arange(local_heads, dtype=jnp.int32)
    ablate = jnp.any(head_ids[:, None] == ablated_heads[None, :], axis=1)
    head_scale = jnp.where(ablate, 0.0, head_mask)

    key_value = lax.all_gather(jnp.stack([keys[0], values[0]]), "ctx", axis=1, tiled=True)
    key_full = key_value[0]
    value_full = key_value[1]

    scores = (
        jnp.einsum("hic,kc->hik", query_heads, key_full, preferred_element_type=jnp.float32)
        * score_scale
    )
    scores = jnp.where(allowed[None], scores, NEG_FILL)
    row_max = jnp.max(scores, axis=-1, keepdims=True)
    exponent = jnp.where(allowed[None], jnp.exp(scores - row_max), 0.0)
    denominator = jnp.sum(exponent, axis=-1, keepdims=True)
    log_total = row_max + jnp.log(denominator)
    weighted = jnp.einsum(
        "hik,kc->hic", exponent.astype(jnp.bfloat16), value_full, preferred_element_type=jnp.float32
    )
    head_out = (weighted / denominator).astype(jnp.bfloat16)
    out_grad = (head_scale[:, None, None] * grad_heads.astype(jnp.float32)).astype(jnp.bfloat16)
    out_dot = jnp.sum(
        out_grad.astype(jnp.float32) * head_out.astype(jnp.float32), axis=-1, keepdims=True
    )
    probability = jnp.where(allowed[None], jnp.exp(scores - log_total), 0.0)
    prob_grad = jnp.einsum(
        "hic,kc->hik", out_grad, value_full, preferred_element_type=jnp.float32
    )
    score_grad = (probability * (prob_grad - out_dot)).astype(jnp.bfloat16)
    value_part = jnp.einsum(
        "hik,hic->kc", probability.astype(jnp.bfloat16), out_grad, preferred_element_type=jnp.float32
    )
    key_part = (
        jnp.einsum("hik,hic->kc", score_grad, query_heads, preferred_element_type=jnp.float32)
        * score_scale
    )
    query_grad = (
        jnp.einsum("hik,kc->hic", score_grad, key_full, preferred_element_type=jnp.float32)
        * score_scale
    ).astype(jnp.bfloat16)
    mask_terms = jnp.sum(
        head_out.astype(jnp.float32) * grad_heads.astype(jnp.float32), axis=(1, 2)
    )

    kv_grad = lax.psum(jnp.stack([key_part, value_part]), "ctx").astype(jnp.bfloat16)
    query_rows = query_grad.transpose(1, 0, 2).reshape(rows_dev, local_heads * DH)
    query_all = lax.all_gather(query_rows, "ctx", axis=0, tiled=True)

    mask_all = lax.all_gather(mask_terms, ("ctx", "rep"), axis=0)
    mask_grad = jnp.sum(mask_all, axis=0) / math.sqrt(lax.axis_size("rep") * seq_len)

    query_piece, key_piece, value_piece = lax.all_gather(
        (w_query, w_key, w_value), "rep", axis=0, tiled=True
    )
    dims = (((1,), (1,)), ((), ()))
    product = lax.dot_general(query_all, query_piece, dims, preferred_element_type=jnp.float32)
    product = product + lax.dot_general(
        kv_grad[0], key_piece, dims, preferred_element_type=jnp.float32
    )
    product = product + lax.dot_general(
        kv_grad[1], value_piece, dims, preferred_element_type=jnp.float32
    )
    partial_value = product.astype(jnp.bfloat16)
    summed = lax.psum_scatter(partial_value, "head", scatter_dimension=1, tiled=True)
    result = summed.reshape(1, seq_len, -1)
    return (result, mask_grad)


def solution(mesh):
    placed = (
        P("rep", "ctx", "head"),
        P("rep", "ctx", "head"),
        P("rep", "ctx", "head"),
        P("rep", "ctx", "head"),
        P("rep", None),
        P("head"),
        P(),
        P(("ctx", "rep"), "head"),
        P(("ctx", "rep"), "head"),
        P(("ctx", "rep"), "head"),
    )
    return jax.shard_map(
        on_device,
        mesh=mesh,
        in_specs=placed,
        out_specs=(P("rep", None, ("ctx", "head")), P("head")),
        check_vma=False,
    )
```

time: 597 us -> 241 us (0.40)
  waiting for transfers between devices: 377 us -> 18.6 us
  blocking collectives: 72.9 us -> 176 us
  starting transfers between devices: 64.8 us -> 0.12 us
  matrix products: 38.4 us -> 16.8 us
  local copies, waits for them, and re-layouts: 22.7 us -> 8.04 us
    unnamed x5 -> x4, waiting for transfers between devices: 197 us -> 18.6 us
    all_gather x3 -> x2, waiting for transfers between devices: 158 us -> 0.01 us  [the longest x1 0.01 us: on_device(): lax.all_gather((w_query, w_key, w_value), 'rep', axis=0, tiled=True)]
    unnamed x0 -> x1, blocking collectives: none -> 73.8 us
    ppermute x24 -> x0, starting transfers between devices: 61.3 us -> none  [shifted(): return lax.ppermute(block, axis, route)]
    all_gather x0 -> x3, blocking collectives: none -> 41.3 us  [the longest x2 25.3 us: on_device(): lax.all_gather((w_query, w_key, w_value), 'rep', axis=0, tiled=True)]
    ppermute x24 -> x0, waiting for transfers between devices: 22.8 us -> none  [shifted(): return lax.ppermute(block, axis, route)]
    dot_general x59 -> x9, matrix products: 38.4 us -> 16.8 us  [the longest x1 4.75 us: on_device(): lax.dot_general(query_all, query_piece, dims, preferred_element_type=jnp....]
    dynamic_slice x17 -> x0, local copies, waits for them, and re-layouts: 12.8 us -> none  [the longest x16 12.2 us: block_source(): lax.dynamic_slice_in_dim(all_seg, key_start, rows_dev, 0)]
  transfers between devices with their start and end apart: 29 -> 3, of which waited for: 20 -> 1; matrix products, arithmetic and copies ran while one was open for 9% -> 8% of each run, Pallas kernels for 0% -> 0%
where the time goes in v1:
time: 241 us; the launch traced here: 239 us
  blocking collectives  176 us (73%)
  waiting for transfers between devices  18.6 us (8%)
  matrix products  16.8 us (7%)
  between operations  14.6 us (6%)
  local copies, waits for them, and re-layouts  8.04 us (3%)
  other arithmetic  4.81 us (2%)
    unnamed x1, blocking collectives  73.8 us
    psum x1, blocking collectives, on_device(): lax.psum(jnp.stack([key_part, value_part]), 'ctx').astype(jnp.bfloat16)  61.3 us
    all_gather x2, blocking collectives, on_device(): lax.all_gather((w_query, w_key, w_value), 'rep', axis=0, tiled=True)  25.3 us
    unnamed x4, waiting for transfers between devices  18.6 us
    all_gather x1, blocking collectives, on_device(): lax.all_gather(jnp.stack([keys[0], values[0]]), 'ctx', axis=1, tiled=True)  16 us
    unnamed x16, local copies, waits for them, and re-layouts  6.22 us
  transfers between devices with their start and end apart: 3, of which 1 were waited for; matrix products, arithmetic and copies ran while one was open for 8% of the time, Pallas kernels for 0%

profile of v1, /device:TPU:4, one launch (start us, length us, event | category | flops | bytes accessed | tf_op | source)
XLA Modules:
  0.0 239.3 jit_solution(772153444491966622)
XLA Ops:
  7.2 0.0 all-gather.6.cloned.1.call-start
  7.2 0.7 all-gather.6.cloned.1.call-update
  7.9 0.0 all-gather.4.cloned.1.call-start
  8.0 0.8 compare_reduce_fusion
  8.8 0.7 dynamic-slice_bitcast_fusion
  9.5 1.0 copy.59
  10.5 1.1 copy.40
  11.6 0.8 pad_maximum_fusion.1
  12.3 0.7 broadcast_select_fusion
  13.0 0.9 fusion.25
  13.9 16.0 %all_gather.21 = bf16[2,1024,128]{2,1,0:T(8,128)(2,1)S(1)} all-gather(bf16[2,128,128]{2,1,0:T(8,128)(2,1)S(1)} %pad_maximum_fusion.1), channel_id=1, replica_groups=mesh['ctx'=8,'head'=8,'rep'=4] {'ctx'}, dimensions={1}, use_global_device_ids=true | all-gather | bytes 589824 | tf_op jit(solution)/shard_map/all_gather | solution.py:37
  29.9 0.7 fusion.3
  30.6 0.0 copy-start
  30.6 1.0 fusion.1
  31.7 1.3 multiply_reduce_fusion
  32.9 0.0 copy-done
  32.9 1.5 multiply_convert_fusion
  34.5 1.2 fusion.15
  35.7 0.0 all-gather.4.cloned.1.call-update
  35.7 0.0 reduce-scatter.4.cloned.1.call-start
  35.7 0.7 fusion.14
  36.4 0.0 copy-start.2
  36.4 0.0 copy-start.3
  36.5 3.3 %fusion.10 = f32[1,1024,128]{2,1,0:T(8,128)S(1)} fusion(bf16[8,128,128]{1,2,0:T(8,128)(2,1)S(1)} %get-tuple-element.4, f32[1024,8,128]{2,0,1:T(8,128)} %copy-done, f32[8,128]{1,0:T(8,128)S(1)} %log_add_fusion, pred[128,1024]{0,1:T(8,128)(4,1)S(1)} %fusion.25), kind=kOutput, calls=%fused_computation.13 | convolution fusion | flops 273678336 | bytes 5115904 | tf_op jit(solution)/shard_map/hik,hic->kc/dot_general | solution.py:63
  39.8 0.1 pad_maximum_fusion
  39.8 0.0 copy-done.2
  39.8 13.1 %all_gather.24 = bf16[1024,128]{1,0:T(8,128)(2,1)S(1)} all-gather(bf16[256,128]{1,0:T(8,128)(2,1)S(1)} %copy-done.2), channel_id=1, replica_groups=mesh['ctx'=8,'head'=8,'rep'=4] {'rep'}, dimensions={0}, use_global_device_ids=true | all-gather | bytes 327680 | tf_op jit(solution)/shard_map/all_gather | solution.py:85
  52.9 0.0 copy-done.3
  52.9 12.2 %all_gather.25 = bf16[1024,128]{1,0:T(8,128)(2,1)S(1)} all-gather(bf16[256,128]{1,0:T(8,128)(2,1)S(1)} %copy-done.3), channel_id=1, replica_groups=mesh['ctx'=8,'head'=8,'rep'=4] {'rep'}, dimensions={0}, use_global_device_ids=true | all-gather | bytes 327680 | tf_op jit(solution)/shard_map/all_gather | solution.py:85
  65.2 61.3 %all-reduce.2 = bf16[2,1024,128]{2,1,0:T(8,128)(2,1)S(1)} all-reduce(f32[2,1024,128]{2,1,0:T(8,128)S(1)} %pad_maximum_fusion), channel_id=1, replica_groups=mesh['ctx'=8,'head'=8,'rep'=4] {'ctx'}, use_global_device_ids=true, to_apply=%region_4.5 | all-reduce | flops 262144 | bytes 1572864 | tf_op jit(solution)/shard_map/psum | solution.py:78
  126.5 2.6 %fusion.26 = f32[1024,1024]{1,0:T(8,128)} fusion(bf16[1024,128]{1,0:T(8,128)(2,1)S(1)} %all_gather.24, bf16[2,1024,128]{2,1,0:T(8,128)(2,1)S(1)} %all-reduce.2), kind=kOutput, calls=%fused_computation.30 | convolution fusion | flops 268435456 | bytes 4718592 | tf_op jit(solution)/shard_map/dot_general | solution.py:90
  129.1 0.0 all-gather.6.cloned.1.call-done
  129.1 0.0 all-gather.4.cloned.1.call-done
  129.1 0.0 copy-start.1
  129.1 4.8 %fusion.38 = f32[1024,1024]{1,0:T(8,128)S(1)} fusion(bf16[1024,1024]{0,1:T(8,128)(2,1)} %all-gather.4.cloned.1.call-done, bf16[1024,1024]{1,0:T(8,128)(2,1)} %all-gather.6.cloned.1.call-done), kind=kOutput, calls=%fused_computation.52 | convolution fusion | flops 2147483648 | bytes 8388608 | tf_op jit(solution)/shard_map/dot_general | solution.py:89
  133.9 0.0 copy-done.1
  133.9 0.7 add_convert_fusion
  134.6 0.0 copy-start.4
  134.6 2.6 %copy.57 = bf16[1024,1024]{0,1:T(8,128)(2,1)} copy(bf16[1024,1024]{1,0:T(8,128)(2,1)S(1)} %add_convert_fusion) | data formatting | bytes 4194304
  137.2 0.0 reduce-scatter.4.cloned.1.call-update
  137.2 0.0 copy-done.4
  137.3 0.6 dynamic-slice.1
  138.5 0.2 dynamic-update-slice
  138.7 73.8 %all-reduce = f32[256]{0:T(256)S(1)} all-reduce(f32[256]{0:T(256)S(1)} %dynamic-update-slice), channel_id=2, replica_groups=mesh['ctx'=8,'head'=8,'rep'=4] {'ctx','rep'}, use_global_device_ids=true, to_apply=%add | all-reduce | flops 256 | bytes 2048
  212.5 0.1 reshape.88
  212.6 0.5 broadcast_multiply_fusion
  213.2 17.9 %reduce-scatter.4.cloned.1.call-done = bf16[128,1024]{1,0:T(8,128)(2,1)} async-done(((bf16[1024,1024]{1,0:T(8,128)(2,1)}), bf16[128,1024]{1,0:T(8,128)(2,1)}) %reduce-scatter.4.cloned.1.call-update) | async-done | bytes 262160
  231.0 1.8 copy.58
  (5 shorter events, 0.0 us)
Async XLA Ops:
  7.2 122.0 %all-gather.6.cloned.1.call-start = ((), (), s32[]{:S(2)}) async-start(), calls=%async_computation.2 | async-start | bytes 2621440 | tf_op jit(solution)/shard_map/all_gather | solution.py:85
  7.9 121.2 %all-gather.4.cloned.1.call-start = ((), (), s32[]{:S(2)}) async-start(), calls=%async_computation.1 | async-start | bytes 2359296 | tf_op jit(solution)/shard_map/all_gather | solution.py:80
  30.6 2.3 copy-start
  35.7 195.3 %reduce-scatter.4.cloned.1.call-start = ((), (), s32[]{:S(2)}) async-start(), calls=%async_computation.3 | async-start | bytes 2359296
  36.4 3.4 %copy-start.2 = (bf16[256,128]{1,0:T(8,128)(2,1)S(1)}, bf16[256,128]{1,0:T(8,128)(2,1)}, u32[]{:S(2)}) copy-start(bf16[256,128]{1,0:T(8,128)(2,1)} %param.18) | copy-start | bytes 196612
  36.4 16.5 %copy-start.3 = (bf16[256,128]{1,0:T(8,128)(2,1)S(1)}, bf16[256,128]{1,0:T(8,128)(2,1)}, u32[]{:S(2)}) copy-start(bf16[256,128]{1,0:T(8,128)(2,1)} %param.19) | copy-start | bytes 196612
  129.1 4.8 %copy-start.1 = (f32[1024,1024]{1,0:T(8,128)S(1)}, f32[1024,1024]{1,0:T(8,128)}, u32[]{:S(2)}) copy-start(f32[1024,1024]{1,0:T(8,128)} %fusion.26) | copy-start | bytes 12582916
  134.6 2.6 %copy-start.4 = (u32[256]{0:T(256)S(1)}, u32[256]{0:T(256)}, u32[]{:S(2)}) copy-start(u32[256]{0:T(256)} %constant.41) | copy-start | bytes 3076
Sparse Core Ops, SparseCore 0:
  9.8 36.7 all-gather.5
  48.9 42.5 all-gather.3
  137.4 93.6 reduce-scatter.3

commit v2 on v1

--- a/solution.py
+++ b/solution.py
@@ -9,6 +9,12 @@
 
 
 NEG_FILL = -1e30
+
+
+def spread(block, axis):
+    count = lax.axis_size(axis)
+    copies = jnp.broadcast_to(block[None], (count,) + block.shape)
+    return lax.all_to_all(copies, axis, 0, 0, tiled=True)
 
 
 def on_device(
@@ -34,9 +40,9 @@
     ablate = jnp.any(head_ids[:, None] == ablated_heads[None, :], axis=1)
     head_scale = jnp.where(ablate, 0.0, head_mask)
 
-    key_value = lax.all_gather(jnp.stack([keys[0], values[0]]), "ctx", axis=1, tiled=True)
-    key_full = key_value[0]
-    value_full = key_value[1]
+    key_value = spread(jnp.stack([keys[0], values[0]]), "ctx")
+    key_full = key_value.transpose(1, 0, 2, 3).reshape(2, seq_len, DH)[0]
+    value_full = key_value.transpose(1, 0, 2, 3).reshape(2, seq_len, DH)[1]
 
     scores = (
         jnp.einsum("hic,kc->hik", query_heads, key_full, preferred_element_type=jnp.float32)
@@ -55,6 +61,12 @@
     out_dot = jnp.sum(
         out_grad.astype(jnp.float32) * head_out.astype(jnp.float32), axis=-1, keepdims=True
     )
+    mask_terms = jnp.sum(
+        head_out.astype(jnp.float32) * grad_heads.astype(jnp.float32), axis=(1, 2)
+    )
+    mask_all = spread(mask_terms, ("ctx", "rep"))
+    mask_grad = jnp.sum(mask_all, axis=0) / math.sqrt(lax.axis_size("rep") * seq_len)
+
     probability = jnp.where(allowed[None], jnp.exp(scores - log_total), 0.0)
     prob_grad = jnp.einsum(
         "hic,kc->hik", out_grad, value_full, preferred_element_type=jnp.float32
@@ -71,30 +83,26 @@
         jnp.einsum("hik,kc->hic", score_grad, key_full, preferred_element_type=jnp.float32)
         * score_scale
     ).astype(jnp.bfloat16)
-    mask_terms = jnp.sum(
-        head_out.astype(jnp.float32) * grad_heads.astype(jnp.float32), axis=(1, 2)
+
+    kv_parts = jnp.concatenate([key_part, value_part], axis=1).reshape(
+        block_count, rows_dev, 2 * DH
     )
+    kv_own = jnp.sum(
+        lax.all_to_all(kv_parts, "ctx", 0, 0, tiled=True), axis=0
+    ).astype(jnp.bfloat16)
+    query_rows = query_grad.transpose(1, 0, 2).reshape(rows_dev, local_heads * DH)
+    grad_rows = jnp.concatenate([query_rows, kv_own], axis=1)
+    grad_all = spread(grad_rows, "ctx").reshape(seq_len, -1)
 
-    kv_grad = lax.psum(jnp.stack([key_part, value_part]), "ctx").astype(jnp.bfloat16)
-    query_rows = query_grad.transpose(1, 0, 2).reshape(rows_dev, local_heads * DH)
-    query_all = lax.all_gather(query_rows, "ctx", axis=0, tiled=True)
-
-    mask_all = lax.all_gather(mask_terms, ("ctx", "rep"), axis=0)
-    mask_grad = jnp.sum(mask_all, axis=0) / math.sqrt(lax.axis_size("rep") * seq_len)
-
-    query_piece, key_piece, value_piece = lax.all_gather(
-        (w_query, w_key, w_value), "rep", axis=0, tiled=True
-    )
-    dims = (((1,), (1,)), ((), ()))
-    product = lax.dot_general(query_all, query_piece, dims, preferred_element_type=jnp.float32)
-    product = product + lax.dot_general(
-        kv_grad[0], key_piece, dims, preferred_element_type=jnp.float32
-    )
-    product = product + lax.dot_general(
-        kv_grad[1], value_piece, dims, preferred_element_type=jnp.float32
-    )
-    partial_value = product.astype(jnp.bfloat16)
-    summed = lax.psum_scatter(partial_value, "head", scatter_dimension=1, tiled=True)
+    weights = jnp.concatenate([w_query, w_key, w_value], axis=1)
+    weight_rows = spread(weights, "rep").reshape(-1, weights.shape[1])
+    heads_count = lax.axis_size("head")
+    weight_rows = weight_rows.reshape(heads_count, -1, weights.shape[1])
+    partial_value = jnp.einsum(
+        "tk,hdk->htd", grad_all, weight_rows, preferred_element_type=jnp.float32
+    ).astype(jnp.bfloat16)
+    arrived = lax.all_to_all(partial_value, "head", 0, 0, tiled=True)
+    summed = jnp.sum(arrived.astype(jnp.float32), axis=0).astype(jnp.bfloat16)
     result = summed.reshape(1, seq_len, -1)
     return (result, mask_grad)
 

time: 241 us -> 238 us (0.988)
  the two profiles are of different devices: /device:TPU:4 before, /device:TPU:32 now
where the time goes in v2:
time: 238 us; the launch traced here: 237 us
  waiting for transfers between devices  113 us (47%)
  blocking collectives  63.8 us (27%)
  starting transfers between devices  31.6 us (13%)
  matrix products  12.7 us (5%)
  local copies, waits for them, and re-layouts  7.82 us (3%)
  other arithmetic  7.27 us (3%)
    all_to_all x1, blocking collectives, spread(): return lax.all_to_all(copies, axis, 0, 0, tiled=True)  63.8 us
    all_to_all x1, waiting for transfers between devices, on_device(): arrived = lax.all_to_all(partial_value, 'head', 0, 0, tiled=True)  52.8 us
    all_to_all x3, waiting for transfers between devices, spread(): return lax.all_to_all(copies, axis, 0, 0, tiled=True)  37.5 us
    all_to_all x1, waiting for transfers between devices, on_device(): lax.all_to_all(kv_parts, 'ctx', 0, 0, tiled=True)  23 us
    all_to_all x3, starting transfers between devices, spread(): return lax.all_to_all(copies, axis, 0, 0, tiled=True)  16.5 us
    all_to_all x1, starting transfers between devices, on_device(): arrived = lax.all_to_all(partial_value, 'head', 0, 0, tiled=True)  8.46 us
    all_to_all x1, starting transfers between devices, on_device(): lax.all_to_all(kv_parts, 'ctx', 0, 0, tiled=True)  6.68 us
    dot_general x1, matrix products, on_device(): jnp.einsum('tk,hdk->htd', grad_all, weight_rows, preferred_element_type=j...  5.88 us
  transfers between devices with their start and end apart: 5, of which 5 were waited for; matrix products, arithmetic and copies ran while one was open for 6% of the time, Pallas kernels for 0%

profile of v2, /device:TPU:32, one launch (start us, length us, event | category | flops | bytes accessed | tf_op | source)
XLA Modules:
  0.0 237.3 jit_solution(7859430715068841578)
XLA Ops:
  0.6 0.8 pad_maximum_fusion.2
  1.4 0.9 broadcast_in_dim.36
  2.3 6.0 %all-to-all-start.1 = ((bf16[8,2,128,128]{3,2,1,0:T(8,128)(2,1)}), bf16[8,2,128,128]{3,2,1,0:T(8,128)(2,1)S(1)}, u32[]{:S(2)}, u32[]{:S(2)}) async-start(bf16[8,2,128,128]{3,2,1,0:T(8,128)(2,1)} %broadcast_in_dim.36), calls=%async_computation.1 | async-start | bytes 1048576 | tf_op jit(solution)/shard_map/all_to_all | solution.py:17
  8.3 1.1 copy.76
  9.4 1.1 copy.54
  10.6 0.7 dynamic-slice_bitcast_fusion
  11.2 0.8 compare_reduce_fusion
  12.1 0.7 broadcast_select_fusion
  12.7 0.9 fusion.24
  13.6 6.8 %all-to-all-done.1 = bf16[8,2,128,128]{3,2,1,0:T(8,128)(2,1)S(1)} async-done(((bf16[8,2,128,128]{3,2,1,0:T(8,128)(2,1)}), bf16[8,2,128,128]{3,2,1,0:T(8,128)(2,1)S(1)}, u32[]{:S(2)}, u32[]{:S(2)}) %all-to-all-start.1) | async-done | bytes 524320 | tf_op jit(solution)/shard_map/all_to_all | solution.py:17
  20.5 0.7 fusion.3
  21.2 1.0 fusion.1
  22.2 1.3 multiply_reduce_fusion
  23.5 1.3 fusion.10
  24.8 1.5 multiply_convert_fusion
  26.3 0.0 copy-start
  26.3 0.0 copy-start.2
  26.3 0.0 copy-start.3
  26.3 0.0 copy-start.4
  26.3 0.8 fusion.13
  27.2 0.5 copy-done
  27.7 1.1 copy_bitcast_fusion
  28.7 6.7 %all-to-all-start.2 = ((f32[8,128,256]{1,2,0:T(8,128)}), f32[8,128,256]{1,2,0:T(8,128)S(1)}, u32[]{:S(2)}, u32[]{:S(2)}) async-start(f32[8,128,256]{1,2,0:T(8,128)} %copy_bitcast_fusion), calls=%async_computation.2 | async-start | bytes 2097152 | tf_op jit(solution)/shard_map/all_to_all | solution.py:91
  35.4 0.0 copy-done.2
  35.4 0.0 copy-done.3
  35.4 0.0 copy-done.4
  35.4 0.1 pad_maximum_fusion
  35.5 23.0 %all-to-all-done.2 = f32[8,128,256]{1,2,0:T(8,128)S(1)} async-done(((f32[8,128,256]{1,2,0:T(8,128)}), f32[8,128,256]{1,2,0:T(8,128)S(1)}, u32[]{:S(2)}, u32[]{:S(2)}) %all-to-all-start.2) | async-done | bytes 1048608 | tf_op jit(solution)/shard_map/all_to_all | solution.py:91
  58.5 1.7 broadcast_in_dim.34
  60.2 0.0 copy-start.1
  60.2 4.7 %all-to-all-start = ((bf16[4,256,1280]{2,1,0:T(8,128)(2,1)}), bf16[4,256,1280]{2,1,0:T(8,128)(2,1)}, u32[]{:S(2)}, u32[]{:S(2)}) async-start(bf16[4,256,1280]{2,1,0:T(8,128)(2,1)} %broadcast_in_dim.34), calls=%async_computation | async-start | bytes 5242880 | tf_op jit(solution)/shard_map/all_to_all | solution.py:17
  64.9 0.0 copy-done.1
  64.9 1.2 fusion.14
  66.1 0.1 reduce_sum.59
  66.1 1.0 pad_maximum_fusion.1
  67.1 0.2 copy.64
  67.3 30.1 %all-to-all-done = bf16[4,256,1280]{2,1,0:T(8,128)(2,1)} async-done(((bf16[4,256,1280]{2,1,0:T(8,128)(2,1)}), bf16[4,256,1280]{2,1,0:T(8,128)(2,1)}, u32[]{:S(2)}, u32[]{:S(2)}) %all-to-all-start) | async-done | bytes 2621472 | tf_op jit(solution)/shard_map/all_to_all | solution.py:17
  97.4 0.2 broadcast_in_dim.68
  97.6 63.8 %all_to_all.31 = bf16[8,128,1280]{2,1,0:T(8,128)(2,1)S(1)} all-to-all(bf16[8,128,1280]{2,1,0:T(8,128)(2,1)S(1)} %broadcast_in_dim.68), channel_id=1, replica_groups=mesh['ctx'=8,'head'=8,'rep'=4] {'ctx'}, dimensions={0} | all-to-all | bytes 5242880 | tf_op jit(solution)/shard_map/all_to_all | solution.py:17
  161.4 0.6 broadcast_in_dim.69
  162.0 5.8 %all-to-all-start.5 = ((f32[32,1,8]{2,1,0:T(1,128)}), f32[32,1,8]{2,1,0:T(1,128)S(1)}, u32[]{:S(2)}, u32[]{:S(2)}) async-start(f32[32,1,8]{2,1,0:T(1,128)} %broadcast_in_dim.69), calls=%async_computation.5 | async-start | bytes 32768 | tf_op jit(solution)/shard_map/all_to_all | solution.py:17
  167.8 5.9 %convert_bitcast_fusion = bf16[8,1024,128]{1,2,0:T(8,128)(2,1)} fusion(bf16[8,128,1280]{2,1,0:T(8,128)(2,1)} %bitcast, bf16[1024,1280,1]{1,0,2:T(8,128)(2,1)S(1)} %bitcast.75), kind=kOutput, calls=%fused_computation.8 | convolution fusion | flops 2685403136 | bytes 7340032 | tf_op jit(solution)/shard_map/tk,hdk->htd/dot_general | solution.py:101
  173.7 0.6 all-to-all-done.5
  174.3 8.5 %all-to-all-start.4 = ((bf16[8,1024,128]{1,2,0:T(8,128)(2,1)}), bf16[8,1024,128]{1,2,0:T(8,128)(2,1)S(1)}, u32[]{:S(2)}, u32[]{:S(2)}) async-start(bf16[8,1024,128]{1,2,0:T(8,128)(2,1)} %convert_bitcast_fusion), calls=%async_computation.4 | async-start | bytes 4194304 | tf_op jit(solution)/shard_map/all_to_all | solution.py:104
  182.7 0.1 reduce_sum.62
  182.8 0.5 broadcast_multiply_fusion
  183.3 52.8 %all-to-all-done.4 = bf16[8,1024,128]{1,2,0:T(8,128)(2,1)S(1)} async-done(((bf16[8,1024,128]{1,2,0:T(8,128)(2,1)}), bf16[8,1024,128]{1,2,0:T(8,128)(2,1)S(1)}, u32[]{:S(2)}, u32[]{:S(2)}) %all-to-all-start.4) | async-done | bytes 2097184 | tf_op jit(solution)/shard_map/all_to_all | solution.py:104
  236.1 0.4 reduce_sum.60
  236.5 0.8 copy.66
  (4 shorter events, 0.1 us)
Async XLA Ops:
  2.3 18.1 %all-to-all-start.1 = ((bf16[8,2,128,128]{3,2,1,0:T(8,128)(2,1)}), bf16[8,2,128,128]{3,2,1,0:T(8,128)(2,1)S(1)}, u32[]{:S(2)}, u32[]{:S(2)}) async-start(bf16[8,2,128,128]{3,2,1,0:T(8,128)(2,1)} %broadcast_in_dim.36), calls=%async_computation.1 | async-start | bytes 1048576 | tf_op jit(solution)/shard_map/all_to_all | solution.py:17
  26.3 1.4 copy-start
  26.3 9.1 %copy-start.2 = (bf16[256,1024]{1,0:T(8,128)(2,1)S(1)}, bf16[256,1024]{1,0:T(8,128)(2,1)}, u32[]{:S(2)}) copy-start(bf16[256,1024]{1,0:T(8,128)(2,1)} %param.17) | copy-start | bytes 1572868
  26.3 9.1 %copy-start.3 = (bf16[256,128]{1,0:T(8,128)(2,1)S(1)}, bf16[256,128]{1,0:T(8,128)(2,1)}, u32[]{:S(2)}) copy-start(bf16[256,128]{1,0:T(8,128)(2,1)} %param.19) | copy-start | bytes 196612
  26.3 9.1 %copy-start.4 = (bf16[256,128]{1,0:T(8,128)(2,1)S(1)}, bf16[256,128]{1,0:T(8,128)(2,1)}, u32[]{:S(2)}) copy-start(bf16[256,128]{1,0:T(8,128)(2,1)} %param.18) | copy-start | bytes 196612
  28.7 29.8 %all-to-all-start.2 = ((f32[8,128,256]{1,2,0:T(8,128)}), f32[8,128,256]{1,2,0:T(8,128)S(1)}, u32[]{:S(2)}, u32[]{:S(2)}) async-start(f32[8,128,256]{1,2,0:T(8,128)} %copy_bitcast_fusion), calls=%async_computation.2 | async-start | bytes 2097152 | tf_op jit(solution)/shard_map/all_to_all | solution.py:91
  60.2 4.7 %copy-start.1 = (bf16[8,128,1024]{1,2,0:T(8,128)(2,1)S(1)}, bf16[8,128,1024]{1,2,0:T(8,128)(2,1)}, u32[]{:S(2)}) copy-start(bf16[8,128,1024]{1,2,0:T(8,128)(2,1)} %copy-done) | copy-start | bytes 6291460
  60.2 37.2 %all-to-all-start = ((bf16[4,256,1280]{2,1,0:T(8,128)(2,1)}), bf16[4,256,1280]{2,1,0:T(8,128)(2,1)}, u32[]{:S(2)}, u32[]{:S(2)}) async-start(bf16[4,256,1280]{2,1,0:T(8,128)(2,1)} %broadcast_in_dim.34), calls=%async_computation | async-start | bytes 5242880 | tf_op jit(solution)/shard_map/all_to_all | solution.py:17
  162.0 12.3 %all-to-all-start.5 = ((f32[32,1,8]{2,1,0:T(1,128)}), f32[32,1,8]{2,1,0:T(1,128)S(1)}, u32[]{:S(2)}, u32[]{:S(2)}) async-start(f32[32,1,8]{2,1,0:T(1,128)} %broadcast_in_dim.69), calls=%async_computation.5 | async-start | bytes 32768 | tf_op jit(solution)/shard_map/all_to_all | solution.py:17
  174.3 61.8 %all-to-all-start.4 = ((bf16[8,1024,128]{1,2,0:T(8,128)(2,1)}), bf16[8,1024,128]{1,2,0:T(8,128)(2,1)S(1)}, u32[]{:S(2)}, u32[]{:S(2)}) async-start(bf16[8,1024,128]{1,2,0:T(8,128)(2,1)} %convert_bitcast_fusion), calls=%async_computation.4 | async-start | bytes 4194304 | tf_op jit(solution)/shard_map/all_to_all | solution.py:104
